TPU v7x, 32 devices: a whole 2x2x4 slice. The times are simulated.
32 devices in a mesh: tm: 8 (over z, x), state: 4 (over y, core).
Axes of the slice: x: 2, y: 2, z: 4, core: 2. Of those that a mesh axis runs over, the one named last changes fastest.
Arguments:
- obs: bfloat16 [2048, 16, 256], P(('state', 'tm')), may hold values from -6 to 6
- mask: int32 [2048, 16], P(('state', 'tm')), may hold values 0 or 1
- loadings: bfloat16 [2048, 2048], P('state'), may hold values from -0.125 to 0.125
- decay: float32 [16, 2048], P('tm', 'state'), may hold values from 0 to 1, as said below
Outputs:
- smoothed: float32 [2048, 16, 256], P('state', 'tm')
- residual: float32 [2048, 16, 256], P('state', 'tm')
Inputs may be any that keep to these rules, and one draw needn't show every extreme that they name: Every decay lies strictly between 0 and 1.
All inputs are finite; a program needn't handle non-finite values. No bound on the sum of `mask` on one device may be relied on, other than what follows from the above.
Results may differ from a plain program's by a relative error of at most 0.0021.
Values may be sent and summed in bfloat16 or wider, within the bound.
No kernel may reach another device: no remote copies, remote signals or barrier semaphores. Data moves between devices by JAX's collectives and lax.ppermute only.
A program may use at most 64 MiB of HBM per device.

v0:
```python
import jax
import jax.numpy as jnp
from jax import lax
from jax.sharding import PartitionSpec as P

CHUNKS = 2


def smooth_chunk(information, decay_all):
    comps, hours, width = information.shape
    state = jnp.zeros((comps, width), jnp.float32)
    filtered = []
    for hour in range(hours):
        state = decay_all[hour][:, None] * state + information[:, hour, :]
        filtered.append(state)
    state = jnp.zeros((comps, width), jnp.float32)
    rows = [None] * hours
    for hour in reversed(range(hours)):
        rate = decay_all[hour]
        state = rate[:, None] * state + (1.0 - rate * rate)[:, None] * filtered[hour]
        rows[hour] = state
    return jnp.stack(rows, axis=1)


def local(obs, mask, loadings, decay):
    tm_count = lax.axis_size("tm")
    tm_index = lax.axis_index("tm")
    _, hours, members = obs.shape
    chunk_members = members // CHUNKS
    masked = obs * mask[:, :, None].astype(obs.dtype)
    by_hour = lax.all_to_all(masked, "tm", split_axis=1, concat_axis=0, tiled=True)
    slab_hours, comps = decay.shape
    padded = jnp.zeros((tm_count, slab_hours, comps), jnp.float32)
    padded = lax.dynamic_update_slice(padded, decay[None], (tm_index, 0, 0))
    decay_all = lax.psum(padded, "tm").reshape(tm_count * slab_hours, comps)
    smoothed_parts = []
    residual_parts = []
    for chunk in range(CHUNKS):
        low = chunk * chunk_members
        piece = masked[:, :, low : low + chunk_members]
        by_member = lax.all_to_all(piece, "tm", split_axis=2, concat_axis=0, tiled=True)
        stations_here, _, width = by_member.shape
        partial = jnp.dot(
            loadings.T,
            by_member.reshape(stations_here, hours * width),
            preferred_element_type=jnp.float32,
        )
        information = lax.psum_scatter(partial, "state", scatter_dimension=0, tiled=True)
        information = information.reshape(information.shape[0], hours, width)
        smoothed_here = smooth_chunk(information, decay_all)
        smoothed = lax.all_to_all(smoothed_here, "tm", split_axis=1, concat_axis=2, tiled=True)
        rounded = smoothed.astype(jnp.bfloat16)
        fitted = jnp.einsum(
            "so,ogy->sgy",
            loadings,
            lax.all_gather(rounded, "state", axis=0, tiled=True),
            preferred_element_type=jnp.float32,
        )
        residual = by_hour[:, :, low : low + chunk_members].astype(jnp.float32) - fitted
        smoothed_parts.append(smoothed)
        residual_parts.append(residual)
    return (jnp.concatenate(smoothed_parts, axis=2), jnp.concatenate(residual_parts, axis=2))


def solution(mesh):
    return jax.shard_map(
        local,
        mesh=mesh,
        in_specs=(
            P(("state", "tm"), None, None),
            P(("state", "tm"), None),
            P("state", None),
            P("tm", "state"),
        ),
        out_specs=(P("state", "tm", None), P("state", "tm", None)),
        check_vma=False,
    )
```

profile of v0, /device:TPU:0, one launch (start us, length us, event | category | flops | bytes accessed | tf_op | source)
XLA Modules:
  0.0 196.1 jit_solution(5214605081453235125)
XLA Ops:
  7.2 0.8 convert_element_type.16
  8.1 3.5 %copy.34 = bf16[64,16,256]{0,1,2:T(8,128)(2,1)} copy(bf16[64,16,256]{2,1,0:T(8,128)(2,1)} %param.4) | data formatting | bytes 1048576 | tf_op args[0]
  11.6 1.3 broadcast_multiply_fusion
  12.9 1.1 fusion.20
  14.0 1.4 reshape.7069
  15.5 16.1 %all_to_all.84 = bf16[8,2,8192]{2,1,0:T(2,128)(2,1)} all-to-all(bf16[8,2,8192]{2,1,0:T(2,128)(2,1)S(1)} %reshape.7069), channel_id=1, replica_groups=mesh['tm'=8,'state'=4] {'tm'}, dimensions={0} | all-to-all | bytes 524288 | tf_op jit(solution)/shard_map/all_to_all | solution.py:41
  31.6 2.1 %reshape.7070 = bf16[128,16,64]{2,1,0:T(8,128)(2,1)} reshape(bf16[8,2,8192]{2,1,0:T(2,128)(2,1)} %all_to_all.84) | data formatting | bytes 524288
  33.7 2.2 %copy.39 = bf16[8,64,16,16]{1,0,3,2:T(8,128)(2,1)} copy(bf16[8,64,16,16]{1,2,3,0:T(8,128)(2,1)} %bitcast.86) | data formatting | bytes 524288 | tf_op jit(solution)/shard_map/all_to_all | solution.py:41
  35.9 1.4 reshape.7066
  37.2 2.0 %convolution_bitcast_fusion = f32[2048,256]{0,1:T(8,128)} fusion(bf16[512,256]{0,1:T(8,128)(2,1)S(1)} %reshape.7066, bf16[512,2048]{1,0:T(8,128)(2,1)S(1)} %copy-done), kind=kOutput, calls=%fused_computation | convolution fusion | flops 536870912 | bytes 4456448 | tf_op jit(solution)/shard_map/dot_general | solution.py:43
  39.4 1.4 reshape.7071
  40.8 12.1 %all_to_all.85 = bf16[8,2,8192]{2,1,0:T(2,128)(2,1)} all-to-all(bf16[8,2,8192]{2,1,0:T(2,128)(2,1)S(1)} %reshape.7071), channel_id=1, replica_groups=mesh['tm'=8,'state'=4] {'tm'}, dimensions={0} | all-to-all | bytes 524288 | tf_op jit(solution)/shard_map/all_to_all | solution.py:41
  52.8 2.1 %reshape.7072 = bf16[128,16,64]{2,1,0:T(8,128)(2,1)} reshape(bf16[8,2,8192]{2,1,0:T(2,128)(2,1)} %all_to_all.85) | data formatting | bytes 524288
  55.0 2.3 %copy.36 = bf16[8,64,16,16]{1,0,3,2:T(8,128)(2,1)} copy(bf16[8,64,16,16]{1,2,3,0:T(8,128)(2,1)} %bitcast.87) | data formatting | bytes 524288 | tf_op jit(solution)/shard_map/all_to_all | solution.py:41
  57.3 1.4 reshape.7064
  58.6 2.1 %convolution_bitcast_fusion.1 = f32[2048,256]{0,1:T(8,128)} fusion(bf16[512,256]{0,1:T(8,128)(2,1)S(1)} %reshape.7064, bf16[512,2048]{1,0:T(8,128)(2,1)S(1)} %copy-done), kind=kOutput, calls=%fused_computation.1 | convolution fusion | flops 536870912 | bytes 4456448 | tf_op jit(solution)/shard_map/dot_general | solution.py:43
  60.8 0.6 copy-done.24
  61.4 35.2 %psum.7 = f32[16,512]{1,0:T(8,128)S(1)} all-reduce(f32[16,512]{1,0:T(8,128)S(1)} %reshape.7063), channel_id=1, replica_groups=mesh['tm'=8,'state'=4] {'tm'}, use_global_device_ids=true, to_apply=%region_0.0 | all-reduce | flops 8192 | bytes 65536 | tf_op jit(solution)/shard_map/psum | solution.py:35
  96.7 0.6 multiply_subtract_fusion.13
  97.3 0.6 multiply_subtract_fusion.11
  97.9 0.6 multiply_subtract_fusion.9
  98.5 0.6 multiply_subtract_fusion.7
  99.1 0.6 multiply_subtract_fusion.5
  99.7 0.6 multiply_subtract_fusion.3
  100.3 0.6 multiply_subtract_fusion.1
  100.9 0.6 broadcast_multiply_fusion.1
  101.6 1.9 constant_dynamic-update-slice_fusion.31
  103.5 0.5 reduce-scatter.3.cloned.1.call-done
  104.0 1.3 constant_dynamic-update-slice_fusion.15
  105.4 1.4 constant_dynamic-update-slice_fusion.14
  106.8 0.6 constant_dynamic-update-slice_fusion.29
  107.4 1.4 constant_dynamic-update-slice_fusion.12
  108.8 0.6 constant_dynamic-update-slice_fusion.27
  109.4 1.3 constant_dynamic-update-slice_fusion.10
  110.7 0.6 constant_dynamic-update-slice_fusion.25
  111.3 0.6 constant_dynamic-update-slice_fusion.8
  112.0 0.6 constant_dynamic-update-slice_fusion.23
  112.6 0.6 constant_dynamic-update-slice_fusion.6
  113.2 0.6 constant_dynamic-update-slice_fusion.21
  113.9 0.6 constant_dynamic-update-slice_fusion.4
  114.5 0.6 constant_dynamic-update-slice_fusion.19
  115.1 1.3 constant_dynamic-update-slice_fusion.2
  116.4 0.6 constant_dynamic-update-slice_fusion.17
  117.0 1.5 constant_dynamic-update-slice_fusion
  118.5 20.1 %all_to_all.86 = f32[512,16,16]{0,2,1:T(8,128)S(1)} all-to-all(f32[512,16,16]{0,2,1:T(8,128)} %get-tuple-element.61), channel_id=1, replica_groups=mesh['tm'=8,'state'=4] {'tm'}, dimensions={1} | all-to-all | bytes 1048576 | tf_op jit(solution)/shard_map/all_to_all | solution.py:51
  138.6 0.8 copy-done.1
  139.4 0.7 bitcast_convert_fusion
  140.2 4.2 %all-to-all-start.1 = ((f32[512,16,16]{0,2,1:T(8,128)}), f32[512,16,16]{0,2,1:T(8,128)}, u32[]{:S(2)}, u32[]{:S(2)}) async-start(f32[512,16,16]{0,2,1:T(8,128)} %copy-done.3), calls=%async_computation.2 | async-start | bytes 1048576 | tf_op jit(solution)/shard_map/all_to_all | solution.py:51
  144.3 1.6 copy.41
  146.0 12.1 %all-to-all-done.1 = f32[512,16,16]{0,2,1:T(8,128)} async-done(((f32[512,16,16]{0,2,1:T(8,128)}), f32[512,16,16]{0,2,1:T(8,128)}, u32[]{:S(2)}, u32[]{:S(2)}) %all-to-all-start.1) | async-done | bytes 524320 | tf_op jit(solution)/shard_map/all_to_all | solution.py:51
  158.0 4.1 %all-to-all-start.4 = ((bf16[64,16,256]{2,0,1:T(8,128)(2,1)}), bf16[64,16,256]{2,0,1:T(8,128)(2,1)}, u32[]{:S(2)}, u32[]{:S(2)}) async-start(bf16[64,16,256]{2,0,1:T(8,128)(2,1)} %copy.41), calls=%async_computation.6 | async-start | bytes 1048576 | tf_op jit(solution)/shard_map/all_to_all | solution.py:31
  162.2 1.1 copy.37
  163.3 0.7 bitcast_convert_fusion.1
  164.1 11.4 %all-to-all-done.4 = bf16[64,16,256]{2,0,1:T(8,128)(2,1)} async-done(((bf16[64,16,256]{2,0,1:T(8,128)(2,1)}), bf16[64,16,256]{2,0,1:T(8,128)(2,1)}, u32[]{:S(2)}, u32[]{:S(2)}) %all-to-all-start.4) | async-done | bytes 524320 | tf_op jit(solution)/shard_map/all_to_all | solution.py:31
  175.5 1.1 copy.42
  176.6 0.8 fusion.21
  177.4 1.8 copy.49
  179.2 0.8 copy.50
  180.1 1.0 pad_maximum_fusion
  181.1 2.2 %copy.45 = f32[512,2,256]{2,1,0:T(2,128)} copy(f32[512,2,256]{0,2,1:T(8,128)} %pad_maximum_fusion) | data formatting | bytes 2097152
  183.4 2.8 %fusion.13 = f32[512,2,128]{0,2,1:T(8,128)} fusion(bf16[2048,2,128]{0,2,1:T(8,128)(2,1)} %all-gather.5.cloned.1.call-done, bf16[512,2048]{1,0:T(8,128)(2,1)S(1)} %copy-done, bf16[512,2,128]{0,2,1:T(8,128)(2,1)S(1)} %copy-done.6), kind=kOutput, calls=%fused_computation.9 | convolution fusion | flops 537133056 | bytes 3932160 | tf_op jit(solution)/shard_map/so,ogy->sgy/dot_general | solution.py:53
  186.2 2.0 %fusion.7 = f32[512,2,128]{0,2,1:T(8,128)S(1)} fusion(bf16[2048,2,128]{0,2,1:T(8,128)(2,1)} %all-gather.3.cloned.1.call-done, bf16[512,2048]{1,0:T(8,128)(2,1)S(1)} %copy-done, bf16[512,2,128]{0,2,1:T(8,128)(2,1)S(1)} %copy-done.5), kind=kOutput, calls=%fused_computation.7 | convolution fusion | flops 537133056 | bytes 3932160 | tf_op jit(solution)/shard_map/so,ogy->sgy/dot_general | solution.py:53
  188.2 0.1 pad_maximum_fusion.1
  188.3 1.3 copy.46
  (71 shorter events, 0.5 us)
Async XLA Ops:
  7.2 30.1 %copy-start = (bf16[512,2048]{1,0:T(8,128)(2,1)S(1)}, bf16[512,2048]{1,0:T(8,128)(2,1)}, u32[]{:S(2)}) copy-start(bf16[512,2048]{1,0:T(8,128)(2,1)} %param.6) | copy-start | bytes 6291460
  7.2 94.3 %reduce-scatter.5.cloned.1.call-start = ((), (), s32[]{:S(2)}) async-start(), calls=%async_computation.8 | async-start | bytes 2621440 | tf_op jit(solution)/shard_map/reduce_scatter | solution.py:48
  39.3 64.7 %reduce-scatter.3.cloned.1.call-start = ((), (), s32[]{:S(2)}) async-start(), calls=%async_computation.7 | async-start | bytes 2621440 | tf_op jit(solution)/shard_map/reduce_scatter | solution.py:48
  60.7 0.7 copy-start.24
  60.7 122.6 %all-gather.5.cloned.1.call-start = ((), (), s32[]{:S(2)}) async-start(), calls=%async_computation.10 | async-start | bytes 1310720 | tf_op jit(solution)/shard_map/all_gather | solution.py:56
  96.6 4.9 %copy-start.7 = (f32[1,512]{1,0:T(1,128)}, f32[1,512]{1,0:T(1,128)S(1)}, u32[]{:S(2)}) copy-start(f32[1,512]{1,0:T(1,128)S(1)} %get-tuple-element.50) | copy-start | bytes 6148
  96.6 4.9 %copy-start.9 = (f32[1,512]{1,0:T(1,128)}, f32[1,512]{1,0:T(1,128)S(1)}, u32[]{:S(2)}) copy-start(f32[1,512]{1,0:T(1,128)S(1)} %get-tuple-element.52) | copy-start | bytes 6148
  96.6 4.9 %copy-start.11 = (f32[1,512]{1,0:T(1,128)}, f32[1,512]{1,0:T(1,128)S(1)}, u32[]{:S(2)}) copy-start(f32[1,512]{1,0:T(1,128)S(1)} %get-tuple-element.54) | copy-start | bytes 6148
  96.7 4.9 %copy-start.12 = (f32[1,512]{1,0:T(1,128)}, f32[1,512]{1,0:T(1,128)S(1)}, u32[]{:S(2)}) copy-start(f32[1,512]{1,0:T(1,128)S(1)} %get-tuple-element.56) | copy-start | bytes 6148
  96.7 4.9 %copy-start.13 = (f32[1,512]{1,0:T(1,128)}, f32[1,512]{1,0:T(1,128)S(1)}, u32[]{:S(2)}) copy-start(f32[1,512]{1,0:T(1,128)S(1)} %get-tuple-element.58) | copy-start | bytes 6148
  96.7 4.9 %copy-start.17 = (f32[1,512]{1,0:T(1,128)}, f32[1,512]{1,0:T(1,128)S(1)}, u32[]{:S(2)}) copy-start(f32[1,512]{1,0:T(1,128)S(1)} %get-tuple-element.47) | copy-start | bytes 6148
  96.7 4.9 %copy-start.18 = (f32[1,512]{1,0:T(1,128)}, f32[1,512]{1,0:T(1,128)S(1)}, u32[]{:S(2)}) copy-start(f32[1,512]{1,0:T(1,128)S(1)} %get-tuple-element.49) | copy-start | bytes 6148
  96.7 4.9 %copy-start.19 = (f32[1,512]{1,0:T(1,128)}, f32[1,512]{1,0:T(1,128)S(1)}, u32[]{:S(2)}) copy-start(f32[1,512]{1,0:T(1,128)S(1)} %get-tuple-element.51) | copy-start | bytes 6148
  96.7 4.9 %copy-start.20 = (f32[1,512]{1,0:T(1,128)}, f32[1,512]{1,0:T(1,128)S(1)}, u32[]{:S(2)}) copy-start(f32[1,512]{1,0:T(1,128)S(1)} %get-tuple-element.53) | copy-start | bytes 6148
  96.7 4.9 %copy-start.21 = (f32[1,512]{1,0:T(1,128)}, f32[1,512]{1,0:T(1,128)S(1)}, u32[]{:S(2)}) copy-start(f32[1,512]{1,0:T(1,128)S(1)} %get-tuple-element.55) | copy-start | bytes 6148
  96.7 4.9 %copy-start.22 = (f32[1,512]{1,0:T(1,128)}, f32[1,512]{1,0:T(1,128)S(1)}, u32[]{:S(2)}) copy-start(f32[1,512]{1,0:T(1,128)S(1)} %get-tuple-element.57) | copy-start | bytes 6148
  96.7 4.9 %copy-start.23 = (f32[1,512]{1,0:T(1,128)}, f32[1,512]{1,0:T(1,128)S(1)}, u32[]{:S(2)}) copy-start(f32[1,512]{1,0:T(1,128)S(1)} %get-tuple-element.59) | copy-start | bytes 6148
  104.0 7.3 %copy-start.10 = (f32[1,512]{1,0:T(1,128)S(1)}, f32[1,512]{1,0:T(1,128)}, u32[]{:S(2)}) copy-start(f32[1,512]{1,0:T(1,128)} %copy-done.9) | copy-start | bytes 6148
  104.0 7.3 %copy-start.16 = (f32[512]{0:T(512)S(1)}, f32[512]{0:T(512)}, u32[]{:S(2)}) copy-start(f32[512]{0:T(512)} %get-tuple-element.86) | copy-start | bytes 6148
  104.0 8.6 %copy-start.8 = (f32[1,512]{1,0:T(1,128)S(1)}, f32[1,512]{1,0:T(1,128)}, u32[]{:S(2)}) copy-start(f32[1,512]{1,0:T(1,128)} %copy-done.7) | copy-start | bytes 6148
  104.0 8.6 %copy-start.15 = (f32[512]{0:T(512)S(1)}, f32[512]{0:T(512)}, u32[]{:S(2)}) copy-start(f32[512]{0:T(512)} %get-tuple-element.88) | copy-start | bytes 6148
  104.0 9.8 %copy-start.14 = (f32[512]{0:T(512)S(1)}, f32[512]{0:T(512)}, u32[]{:S(2)}) copy-start(f32[512]{0:T(512)} %get-tuple-element.90) | copy-start | bytes 6148
  118.5 20.1 %copy-start.3 = (f32[512,16,16]{0,2,1:T(8,128)}, f32[512,16,16]{0,2,1:T(8,128)S(1)}, u32[]{:S(2)}) copy-start(f32[512,16,16]{0,2,1:T(8,128)S(1)} %get-tuple-element.60) | copy-start | bytes 1572868
  138.6 0.8 copy-start.1
  140.2 17.9 %all-to-all-start.1 = ((f32[512,16,16]{0,2,1:T(8,128)}), f32[512,16,16]{0,2,1:T(8,128)}, u32[]{:S(2)}, u32[]{:S(2)}) async-start(f32[512,16,16]{0,2,1:T(8,128)} %copy-done.3), calls=%async_computation.2 | async-start | bytes 1048576 | tf_op jit(solution)/shard_map/all_to_all | solution.py:51
  158.0 17.5 %all-to-all-start.4 = ((bf16[64,16,256]{2,0,1:T(8,128)(2,1)}), bf16[64,16,256]{2,0,1:T(8,128)(2,1)}, u32[]{:S(2)}, u32[]{:S(2)}) async-start(bf16[64,16,256]{2,0,1:T(8,128)(2,1)} %copy.41), calls=%async_computation.6 | async-start | bytes 1048576 | tf_op jit(solution)/shard_map/all_to_all | solution.py:31
  162.2 24.0 %all-gather.3.cloned.1.call-start = ((), (), s32[]{:S(2)}) async-start(), calls=%async_computation.9 | async-start | bytes 1310720 | tf_op jit(solution)/shard_map/all_gather | solution.py:56
  163.3 16.7 %copy-start.2 = (f32[512,8,2,16]{0,3,1,2:T(8,128)S(1)}, f32[512,8,2,16]{0,3,1,2:T(8,128)}, u32[]{:S(2)}) copy-start(f32[512,8,2,16]{0,3,1,2:T(8,128)} %copy-done.1) | copy-start | bytes 1572868
  180.1 3.3 %copy-start.6 = (bf16[512,2,128]{0,2,1:T(8,128)(2,1)S(1)}, bf16[512,2,128]{0,2,1:T(8,128)(2,1)}, u32[]{:S(2)}) copy-start(bf16[512,2,128]{0,2,1:T(8,128)(2,1)} %copy.50) | copy-start | bytes 786436
  183.3 2.8 %copy-start.5 = (bf16[512,2,128]{0,2,1:T(8,128)(2,1)S(1)}, bf16[512,2,128]{0,2,1:T(8,128)(2,1)}, u32[]{:S(2)}) copy-start(bf16[512,2,128]{0,2,1:T(8,128)(2,1)} %copy.49) | copy-start | bytes 786436
  186.2 2.0 %copy-start.4 = (f32[512,2,128]{0,2,1:T(8,128)S(1)}, f32[512,2,128]{0,2,1:T(8,128)}, u32[]{:S(2)}) copy-start(f32[512,2,128]{0,2,1:T(8,128)} %fusion.13) | copy-start | bytes 1572868
Sparse Core Ops, SparseCore 0:
  39.4 30.4 reduce-scatter.4
  72.6 31.3 reduce-scatter.2
  140.3 14.7 all-gather.4
  164.3 17.0 all-gather.2
where the time goes:
time: 198 us; the launch traced here: 196 us
  blocking collectives  83.4 us (42%)
  local copies, waits for them, and re-layouts  35.7 us (18%)
  waiting for transfers between devices  24.1 us (12%)
  other arithmetic  21.4 us (11%)
  between operations  14.1 us (7%)
  matrix products  8.94 us (5%)
  starting transfers between devices  8.46 us (4%)
    psum x1, blocking collectives, local(): decay_all = lax.psum(padded, 'tm').reshape(tm_count * slab_hours, comps)  35.2 us
    all_to_all x2, blocking collectives, local(): lax.all_to_all(piece, 'tm', split_axis=2, concat_axis=0, tiled=True)  28.1 us
    unnamed x73, local copies, waits for them, and re-layouts  22.7 us
    all_to_all x1, blocking collectives, local(): lax.all_to_all(smoothed_here, 'tm', split_axis=1, concat_axis=2, tiled=True)  20.1 us
    all_to_all x1, waiting for transfers between devices, local(): lax.all_to_all(smoothed_here, 'tm', split_axis=1, concat_axis=2, tiled=True)  12.1 us
    all_to_all x1, waiting for transfers between devices, local(): lax.all_to_all(masked, 'tm', split_axis=1, concat_axis=0, tiled=True)  11.4 us
    unnamed x9, other arithmetic  10.5 us
    dot_general x2, matrix products, local(): jnp.einsum('so,ogy->sgy', loadings, lax.all_gather(rounded, 'state', axis...  4.83 us
  transfers between devices with their start and end apart: 6, of which 3 were waited for; matrix products, arithmetic and copies ran while one was open for 15% of the time, Pallas kernels for 0%

commit v1 on v0

--- a/solution.py
+++ b/solution.py
@@ -48,7 +48,12 @@
         information = lax.psum_scatter(partial, "state", scatter_dimension=0, tiled=True)
         information = information.reshape(information.shape[0], hours, width)
         smoothed_here = smooth_chunk(information, decay_all)
-        smoothed = lax.all_to_all(smoothed_here, "tm", split_axis=1, concat_axis=2, tiled=True)
+        smoothed = jnp.concatenate(
+            lax.all_to_all(
+                jnp.stack(jnp.split(smoothed_here, lax.axis_size("tm"), axis=1), axis=0), "tm", 0, 0
+            ),
+            2,
+        )
         rounded = smoothed.astype(jnp.bfloat16)
         fitted = jnp.einsum(
             "so,ogy->sgy",

time: 198 us -> 178 us (0.90)
  blocking collectives: 83.4 us -> 63.3 us
  starting transfers between devices: 8.46 us -> 15.2 us
  local copies, waits for them, and re-layouts: 35.7 us -> 32.4 us
  other arithmetic: 21.4 us -> 19.2 us
    all_to_all x1 -> x0, blocking collectives: 20.1 us -> none  [local(): lax.all_to_all(smoothed_here, 'tm', split_axis=1, concat_axis=2, tiled=True)]
    add x0 -> x4, other arithmetic: none -> 4.35 us  [the longest x2 2.28 us: smooth_chunk(): rate[:, None] * state + (1.0 - rate * rate)[:, None] * filtered[hour]]
    unnamed x73 -> x23, local copies, waits for them, and re-layouts: 22.7 us -> 18.3 us
    all_to_all x1 -> x2, starting transfers between devices: 4.15 us -> 8.29 us  [local(): lax.all_to_all(jnp.stack(jnp.split(smoothed_here, lax.axis_size('tm'), ax...]
    sub x7, other arithmetic: 4.14 us -> 0.04 us  [smooth_chunk(): 1.0 - rate * rate]
    all_to_all x1 -> x2, waiting for transfers between devices: 12.1 us -> 15.2 us  [local(): lax.all_to_all(jnp.stack(jnp.split(smoothed_here, lax.axis_size('tm'), ax...]
    all_to_all x1, waiting for transfers between devices: 11.4 us -> 8.48 us  [local(): lax.all_to_all(masked, 'tm', split_axis=1, concat_axis=0, tiled=True)]
    all_to_all x1, starting transfers between devices: 4.14 us -> 6.73 us  [local(): lax.all_to_all(masked, 'tm', split_axis=1, concat_axis=0, tiled=True)]
  transfers between devices with their start and end apart: 6 -> 7, of which waited for: 3 -> 3; matrix products, arithmetic and copies ran while one was open for 15% -> 21% of each run, Pallas kernels for 0% -> 0%
where the time goes in v1:
time: 178 us; the launch traced here: 177 us
  blocking collectives  63.3 us (36%)
  local copies, waits for them, and re-layouts  32.4 us (18%)
  waiting for transfers between devices  23.7 us (13%)
  other arithmetic  19.2 us (11%)
  starting transfers between devices  15.2 us (9%)
  between operations  14 us (8%)
  matrix products  8.93 us (5%)
    psum x1, blocking collectives, local(): decay_all = lax.psum(padded, 'tm').reshape(tm_count * slab_hours, comps)  35.2 us
    all_to_all x2, blocking collectives, local(): lax.all_to_all(piece, 'tm', split_axis=2, concat_axis=0, tiled=True)  28.1 us
    unnamed x23, local copies, waits for them, and re-layouts  18.3 us
    all_to_all x2, waiting for transfers between devices, local(): lax.all_to_all(jnp.stack(jnp.split(smoothed_here, lax.axis_size('tm'), ax...  15.2 us
    unnamed x14, other arithmetic  8.88 us
    all_to_all x1, waiting for transfers between devices, local(): lax.all_to_all(masked, 'tm', split_axis=1, concat_axis=0, tiled=True)  8.48 us
    all_to_all x2, starting transfers between devices, local(): lax.all_to_all(jnp.stack(jnp.split(smoothed_here, lax.axis_size('tm'), ax...  8.29 us
    all_to_all x1, starting transfers between devices, local(): lax.all_to_all(masked, 'tm', split_axis=1, concat_axis=0, tiled=True)  6.73 us
  transfers between devices with their start and end apart: 7, of which 3 were waited for; matrix products, arithmetic and copies ran while one was open for 21% of the time, Pallas kernels for 0%

profile of v1, /device:TPU:0, one launch (start us, length us, event | category | flops | bytes accessed | tf_op | source)
XLA Modules:
  0.0 176.8 jit_solution(11815488177007322028)
XLA Ops:
  7.2 0.0 reduce-scatter.5.cloned.1.call-start
  7.2 0.8 convert_element_type.16
  8.1 3.5 %copy.34 = bf16[64,16,256]{0,1,2:T(8,128)(2,1)} copy(bf16[64,16,256]{2,1,0:T(8,128)(2,1)} %param.4) | data formatting | bytes 1048576 | tf_op args[0]
  11.6 1.3 broadcast_multiply_fusion
  12.9 1.1 fusion.38
  14.0 1.4 reshape.7085
  15.5 16.1 %all_to_all.58 = bf16[8,2,8192]{2,1,0:T(2,128)(2,1)} all-to-all(bf16[8,2,8192]{2,1,0:T(2,128)(2,1)S(1)} %reshape.7085), channel_id=1, replica_groups=mesh['tm'=8,'state'=4] {'tm'}, dimensions={0} | all-to-all | bytes 524288 | tf_op jit(solution)/shard_map/all_to_all | solution.py:41
  31.6 2.1 %reshape.7086 = bf16[128,16,64]{2,1,0:T(8,128)(2,1)} reshape(bf16[8,2,8192]{2,1,0:T(2,128)(2,1)} %all_to_all.58) | data formatting | bytes 524288
  33.7 2.2 %copy.39 = bf16[8,64,16,16]{1,0,3,2:T(8,128)(2,1)} copy(bf16[8,64,16,16]{1,2,3,0:T(8,128)(2,1)} %bitcast.146) | data formatting | bytes 524288 | tf_op jit(solution)/shard_map/all_to_all | solution.py:41
  35.9 1.4 reshape.7080
  37.3 2.1 %convolution_bitcast_fusion = f32[2048,256]{0,1:T(8,128)} fusion(bf16[512,256]{0,1:T(8,128)(2,1)S(1)} %reshape.7080, bf16[512,2048]{1,0:T(8,128)(2,1)S(1)} %copy-done), kind=kOutput, calls=%fused_computation | convolution fusion | flops 536870912 | bytes 4456448 | tf_op jit(solution)/shard_map/dot_general | solution.py:43
  39.4 0.0 reduce-scatter.3.cloned.1.call-start
  39.4 1.4 reshape.7087
  40.8 12.1 %all_to_all.59 = bf16[8,2,8192]{2,1,0:T(2,128)(2,1)} all-to-all(bf16[8,2,8192]{2,1,0:T(2,128)(2,1)S(1)} %reshape.7087), channel_id=1, replica_groups=mesh['tm'=8,'state'=4] {'tm'}, dimensions={0} | all-to-all | bytes 524288 | tf_op jit(solution)/shard_map/all_to_all | solution.py:41
  52.9 2.1 %reshape.7088 = bf16[128,16,64]{2,1,0:T(8,128)(2,1)} reshape(bf16[8,2,8192]{2,1,0:T(2,128)(2,1)} %all_to_all.59) | data formatting | bytes 524288
  55.0 2.3 %copy.36 = bf16[8,64,16,16]{1,0,3,2:T(8,128)(2,1)} copy(bf16[8,64,16,16]{1,2,3,0:T(8,128)(2,1)} %bitcast.147) | data formatting | bytes 524288 | tf_op jit(solution)/shard_map/all_to_all | solution.py:41
  57.3 1.4 reshape.7076
  58.7 2.0 %convolution_bitcast_fusion.1 = f32[2048,256]{0,1:T(8,128)} fusion(bf16[512,256]{0,1:T(8,128)(2,1)S(1)} %reshape.7076, bf16[512,2048]{1,0:T(8,128)(2,1)S(1)} %copy-done), kind=kOutput, calls=%fused_computation.1 | convolution fusion | flops 536870912 | bytes 4456448 | tf_op jit(solution)/shard_map/dot_general | solution.py:43
  60.8 0.6 copy-done.6
  61.4 35.2 %psum.7 = f32[16,512]{1,0:T(8,128)S(1)} all-reduce(f32[16,512]{1,0:T(8,128)S(1)} %reshape.7075), channel_id=1, replica_groups=mesh['tm'=8,'state'=4] {'tm'}, use_global_device_ids=true, to_apply=%region_0.0 | all-reduce | flops 8192 | bytes 65536 | tf_op jit(solution)/shard_map/psum | solution.py:35
  96.8 1.0 slice_add_fusion.2
  97.8 1.1 multiply_add_fusion
  98.9 0.6 fusion.24
  99.6 0.6 fusion.25
  100.2 0.6 fusion.26
  100.8 0.6 fusion.27
  101.5 0.6 fusion.28
  102.1 0.6 fusion.29
  102.8 0.6 fusion.30
  103.4 0.6 fusion.31
  104.0 4.1 %all-to-all-start.3 = ((f32[8,512,2,16]{1,3,2,0:T(8,128)}), f32[8,512,2,16]{1,3,2,0:T(8,128)}, u32[]{:S(2)}, u32[]{:S(2)}) async-start(f32[8,512,2,16]{1,3,2,0:T(8,128)} %fusion.31), calls=%async_computation.5 | async-start | bytes 1048576 | tf_op jit(solution)/shard_map/all_to_all | solution.py:52
  108.2 0.0 all-gather.5.cloned.1.call-start
  108.2 1.0 slice_add_fusion.18
  109.3 1.1 multiply_add_fusion.15
  110.4 0.6 fusion.16
  111.0 0.6 fusion.17
  111.7 0.6 fusion.18
  112.3 0.6 fusion.19
  113.0 5.5 %all-to-all-done.3 = f32[8,512,2,16]{1,3,2,0:T(8,128)} async-done(((f32[8,512,2,16]{1,3,2,0:T(8,128)}), f32[8,512,2,16]{1,3,2,0:T(8,128)}, u32[]{:S(2)}, u32[]{:S(2)}) %all-to-all-start.3) | async-done | bytes 524320 | tf_op jit(solution)/shard_map/all_to_all | solution.py:52
  118.5 1.1 copy.40
  119.5 0.8 copy-done.1
  120.3 0.7 bitcast_convert_fusion
  121.1 0.6 fusion.20
  121.7 0.6 fusion.21
  122.4 0.6 fusion.22
  123.0 0.6 fusion.23
  123.6 4.1 %all-to-all-start.1 = ((f32[8,512,2,16]{1,3,2,0:T(8,128)}), f32[8,512,2,16]{1,3,2,0:T(8,128)}, u32[]{:S(2)}, u32[]{:S(2)}) async-start(f32[8,512,2,16]{1,3,2,0:T(8,128)} %fusion.23), calls=%async_computation.2 | async-start | bytes 1048576 | tf_op jit(solution)/shard_map/all_to_all | solution.py:52
  127.8 1.6 copy.41
  129.4 9.7 %all-to-all-done.1 = f32[8,512,2,16]{1,3,2,0:T(8,128)} async-done(((f32[8,512,2,16]{1,3,2,0:T(8,128)}), f32[8,512,2,16]{1,3,2,0:T(8,128)}, u32[]{:S(2)}, u32[]{:S(2)}) %all-to-all-start.1) | async-done | bytes 524320 | tf_op jit(solution)/shard_map/all_to_all | solution.py:52
  139.1 6.7 %all-to-all-start.4 = ((bf16[64,16,256]{2,0,1:T(8,128)(2,1)}), bf16[64,16,256]{2,0,1:T(8,128)(2,1)}, u32[]{:S(2)}, u32[]{:S(2)}) async-start(bf16[64,16,256]{2,0,1:T(8,128)(2,1)} %copy.41), calls=%async_computation.6 | async-start | bytes 1048576 | tf_op jit(solution)/shard_map/all_to_all | solution.py:31
  145.8 0.0 all-gather.3.cloned.1.call-start
  145.9 1.1 copy.37
  147.0 0.7 bitcast_convert_fusion.1
  147.7 8.5 %all-to-all-done.4 = bf16[64,16,256]{2,0,1:T(8,128)(2,1)} async-done(((bf16[64,16,256]{2,0,1:T(8,128)(2,1)}), bf16[64,16,256]{2,0,1:T(8,128)(2,1)}, u32[]{:S(2)}, u32[]{:S(2)}) %all-to-all-start.4) | async-done | bytes 524320 | tf_op jit(solution)/shard_map/all_to_all | solution.py:31
  156.2 1.1 copy.42
  157.3 0.8 fusion.39
  158.1 1.8 %copy.49 = bf16[512,2,128]{0,2,1:T(8,128)(2,1)} copy(bf16[512,2,128]{2,0,1:T(8,128)(2,1)} %get-tuple-element.58) | data formatting | bytes 524288
  159.9 0.9 copy.50
  160.7 1.0 pad_maximum_fusion
  161.8 2.3 %copy.45 = f32[512,2,256]{2,1,0:T(2,128)} copy(f32[512,2,256]{0,2,1:T(8,128)} %pad_maximum_fusion) | data formatting | bytes 2097152
  164.0 2.8 %fusion.13 = f32[512,2,128]{0,2,1:T(8,128)} fusion(bf16[2048,2,128]{0,2,1:T(8,128)(2,1)} %all-gather.5.cloned.1.call-done, bf16[512,2048]{1,0:T(8,128)(2,1)S(1)} %copy-done, bf16[512,2,128]{0,2,1:T(8,128)(2,1)S(1)} %copy-done.5), kind=kOutput, calls=%fused_computation.9 | convolution fusion | flops 537133056 | bytes 3932160 | tf_op jit(solution)/shard_map/so,ogy->sgy/dot_general | solution.py:58
  166.9 2.0 %fusion.7 = f32[512,2,128]{0,2,1:T(8,128)S(1)} fusion(bf16[2048,2,128]{0,2,1:T(8,128)(2,1)} %all-gather.3.cloned.1.call-done, bf16[512,2048]{1,0:T(8,128)(2,1)S(1)} %copy-done, bf16[512,2,128]{0,2,1:T(8,128)(2,1)S(1)} %copy-done.4), kind=kOutput, calls=%fused_computation.7 | convolution fusion | flops 537133056 | bytes 3932160 | tf_op jit(solution)/shard_map/so,ogy->sgy/dot_general | solution.py:58
  168.9 0.1 pad_maximum_fusion.1
  169.0 1.3 copy.46
  (32 shorter events, 0.3 us)
Async XLA Ops:
  7.2 30.1 %copy-start = (bf16[512,2048]{1,0:T(8,128)(2,1)S(1)}, bf16[512,2048]{1,0:T(8,128)(2,1)}, u32[]{:S(2)}) copy-start(bf16[512,2048]{1,0:T(8,128)(2,1)} %param.6) | copy-start | bytes 6291460
  7.2 89.6 %reduce-scatter.5.cloned.1.call-start = ((), (), s32[]{:S(2)}) async-start(), calls=%async_computation.8 | async-start | bytes 2621440 | tf_op jit(solution)/shard_map/reduce_scatter | solution.py:48
  39.4 68.9 %reduce-scatter.3.cloned.1.call-start = ((), (), s32[]{:S(2)}) async-start(), calls=%async_computation.7 | async-start | bytes 2621440 | tf_op jit(solution)/shard_map/reduce_scatter | solution.py:48
  60.7 0.7 copy-start.6
  104.0 14.4 %all-to-all-start.3 = ((f32[8,512,2,16]{1,3,2,0:T(8,128)}), f32[8,512,2,16]{1,3,2,0:T(8,128)}, u32[]{:S(2)}, u32[]{:S(2)}) async-start(f32[8,512,2,16]{1,3,2,0:T(8,128)} %fusion.31), calls=%async_computation.5 | async-start | bytes 1048576 | tf_op jit(solution)/shard_map/all_to_all | solution.py:52
  108.2 55.9 %all-gather.5.cloned.1.call-start = ((), (), s32[]{:S(2)}) async-start(), calls=%async_computation.10 | async-start | bytes 1310720 | tf_op jit(solution)/shard_map/all_gather | solution.py:61
  119.5 0.8 copy-start.1
  123.6 15.5 %all-to-all-start.1 = ((f32[8,512,2,16]{1,3,2,0:T(8,128)}), f32[8,512,2,16]{1,3,2,0:T(8,128)}, u32[]{:S(2)}, u32[]{:S(2)}) async-start(f32[8,512,2,16]{1,3,2,0:T(8,128)} %fusion.23), calls=%async_computation.2 | async-start | bytes 1048576 | tf_op jit(solution)/shard_map/all_to_all | solution.py:52
  139.1 17.1 %all-to-all-start.4 = ((bf16[64,16,256]{2,0,1:T(8,128)(2,1)}), bf16[64,16,256]{2,0,1:T(8,128)(2,1)}, u32[]{:S(2)}, u32[]{:S(2)}) async-start(bf16[64,16,256]{2,0,1:T(8,128)(2,1)} %copy.41), calls=%async_computation.6 | async-start | bytes 1048576 | tf_op jit(solution)/shard_map/all_to_all | solution.py:31
  145.8 21.0 %all-gather.3.cloned.1.call-start = ((), (), s32[]{:S(2)}) async-start(), calls=%async_computation.9 | async-start | bytes 1310720 | tf_op jit(solution)/shard_map/all_gather | solution.py:61
  146.9 13.8 %copy-start.2 = (f32[512,2,8,16]{0,3,2,1:T(8,128)S(1)}, f32[512,2,8,16]{0,3,2,1:T(8,128)}, u32[]{:S(2)}) copy-start(f32[512,2,8,16]{0,3,2,1:T(8,128)} %copy-done.1) | copy-start | bytes 1572868
  160.7 3.3 %copy-start.5 = (bf16[512,2,128]{0,2,1:T(8,128)(2,1)S(1)}, bf16[512,2,128]{0,2,1:T(8,128)(2,1)}, u32[]{:S(2)}) copy-start(bf16[512,2,128]{0,2,1:T(8,128)(2,1)} %copy.50) | copy-start | bytes 786436
  164.0 2.8 %copy-start.4 = (bf16[512,2,128]{0,2,1:T(8,128)(2,1)S(1)}, bf16[512,2,128]{0,2,1:T(8,128)(2,1)}, u32[]{:S(2)}) copy-start(bf16[512,2,128]{0,2,1:T(8,128)(2,1)} %copy.49) | copy-start | bytes 786436
  166.9 2.0 %copy-start.3 = (f32[512,2,128]{0,2,1:T(8,128)S(1)}, f32[512,2,128]{0,2,1:T(8,128)}, u32[]{:S(2)}) copy-start(f32[512,2,128]{0,2,1:T(8,128)} %fusion.13) | copy-start | bytes 1572868
Sparse Core Ops, SparseCore 0:
  39.5 30.4 reduce-scatter.4
  72.6 31.3 reduce-scatter.2
  121.2 15.8 all-gather.4
  147.9 18.3 all-gather.2
